TPU v7x, 256 devices: a whole 4x4x8 slice. The times are simulated.
256 devices in a mesh: gx: 4 (over x), gy: 8 (over z_hi, core), gz: 8 (over z_lo, y).
Axes of the slice: x: 4, y: 4, z: 8 (z_hi: 4, z_lo: 2; z = z_hi * 2 + z_lo), core: 2. Of those that a mesh axis runs over, the one named last changes fastest.
Arguments:
- fine: float32 [5, 64, 128, 1024], P(None, 'gx', 'gy', 'gz'), as said below
- shell: float32 [4, 512, 3840], P('gx', ('gy', 'gz')), as said below
- parent: int32 [4, 512], P('gx'), may hold values from 0 to 511, as said below
- link: int32 [6, 4, 8, 64], P(None, 'gx', 'gy', 'gz'), may hold values 0 or 1
Outputs:
- fine_new: float32 [5, 64, 128, 1024], P(None, 'gx', 'gy', 'gz')
- coarse_new: float32 [4, 512, 2560], P('gx', ('gy', 'gz'))
Inputs may be any that keep to these rules, and one draw needn't show every extreme that they name: Each row parent[i, :] names every slot 0 to 511 exactly once. Of the 8 blocks q = d * 8 to d * 8 + 7 of a row, at most 2 have parents among the slots o * 8 to o * 8 + 7 of any one o, and every such pair that meets at all holds exactly 2. `fine`: density and energy make pressure positive in every cell; velocities stay well below the sound speed times a few. `shell`: same physical ranges as fine.
All inputs are finite; a program needn't handle non-finite values. No bound on the sum of `link` on one device may be relied on, other than what follows from the above.
Results may differ from a plain program's by a relative error of at most 0.0003.
Values sent between devices are 32-bit elements; how exact they have to be, the bound alone decides.
No kernel may reach another device: no remote copies, remote signals or barrier semaphores. Data moves between devices by JAX's collectives and lax.ppermute only.
A program may use at most 128 MiB of HBM per device.

v0:
```python
import jax
import jax.numpy as jnp
from jax import lax
from jax.sharding import PartitionSpec as P

BS = 16
GAMMA = 1.4
LAMBDA = 0.05


def padded_2(cells, sides, width):
    for axis, dim in sides:
        count = lax.axis_size(axis)
        head = lax.slice_in_dim(cells, 0, width, axis=dim)
        tail = lax.slice_in_dim(cells, cells.shape[dim] - width, cells.shape[dim], axis=dim)
        cells = jnp.concatenate(
            [
                lax.ppermute(tail, axis, [(i, (i + 1) % count) for i in range(count)]),
                cells,
                lax.ppermute(head, axis, [((i + 1) % count, i) for i in range(count)]),
            ],
            axis=dim,
        )
    return cells


def cell_flux(state, direc):
    rho = state[0]
    mom = state[1:4]
    energy = state[4]
    vel = mom / rho[None]
    press = (GAMMA - 1.0) * (energy - 0.5 * jnp.sum(mom * vel, axis=0))
    normal = vel[direc]
    parts = [
        mom[direc],
        mom[0] * normal,
        mom[1] * normal,
        mom[2] * normal,
        (energy + press) * normal,
    ]
    parts[1 + direc] = parts[1 + direc] + press
    flux = jnp.stack(parts, axis=0)
    speed = jnp.abs(normal) + jnp.sqrt(GAMMA * press / rho)
    return (flux, speed)


def pair_face(flux_a, speed_a, value_a, flux_b, speed_b, value_b):
    return 0.5 * (flux_a + flux_b) - 0.5 * jnp.maximum(speed_a, speed_b)[None] * (value_b - value_a)


def along_axis(ext, direc):
    flux, speed = cell_flux(ext, direc)
    dim = 1 + direc
    count = ext.shape[dim]
    face = pair_face(
        lax.slice_in_dim(flux, 0, count - 1, axis=dim),
        lax.slice_in_dim(speed, 0, count - 1, axis=dim - 1),
        lax.slice_in_dim(ext, 0, count - 1, axis=dim),
        lax.slice_in_dim(flux, 1, count, axis=dim),
        lax.slice_in_dim(speed, 1, count, axis=dim - 1),
        lax.slice_in_dim(ext, 1, count, axis=dim),
    )
    return lax.slice_in_dim(face, 1, count - 1, axis=dim) - lax.slice_in_dim(
        face, 0, count - 2, axis=dim
    )


def along_blocks(state, ghost_low, ghost_high):
    nz_dev = state.shape[3]
    flux, speed = cell_flux(state, 2)
    inner = pair_face(
        jnp.roll(flux, 1, axis=3),
        jnp.roll(speed, 1, axis=2),
        jnp.roll(state, 1, axis=3),
        flux,
        speed,
        state,
    )
    low_flux, low_speed = cell_flux(ghost_low, 2)
    high_flux, high_speed = cell_flux(ghost_high, 2)
    start = pair_face(
        low_flux, low_speed, ghost_low, flux[..., 0::BS], speed[..., 0::BS], state[..., 0::BS]
    )
    finish = pair_face(
        flux[..., BS - 1 :: BS],
        speed[..., BS - 1 :: BS],
        state[..., BS - 1 :: BS],
        high_flux,
        high_speed,
        ghost_high,
    )
    plane = jnp.arange(nz_dev, dtype=jnp.int32) % BS
    left_face = jnp.where(plane == 0, jnp.repeat(start, BS, axis=3), inner)
    right_face = jnp.where(
        plane == BS - 1, jnp.repeat(finish, BS, axis=3), jnp.roll(left_face, -1, axis=3)
    )
    return right_face - left_face


def inject(coarse):
    return jnp.repeat(jnp.repeat(coarse, 2, axis=-2), 2, axis=-1)


def side_ghost(fine_face, level, links, face, nz_dev):
    coarse = inject(level[:, face]).transpose(1, 2, 0, 3).reshape(5, BS, nz_dev)
    chosen = jnp.repeat(links[:, face] == 1, BS)[None, None, :]
    return jnp.where(chosen, fine_face, coarse)


def end_ghost(fine_face, level, links, face):
    coarse = inject(level[:, face]).transpose(1, 2, 3, 0)
    chosen = (links[:, face] == 1)[None, None, None, :]
    return jnp.where(chosen, fine_face, coarse)


def restrict_state(state, nblk):
    half = BS // 2
    grouped = state.reshape(5, half, 2, half, 2, nblk, half, 2)
    means = grouped.mean(axis=(2, 4, 7))
    return means.transpose(3, 0, 1, 2, 4).reshape(nblk, -1)


def shards(fine, shell, parent, link):
    half = BS // 2
    nz_dev = fine.shape[3]
    nblk = nz_dev // BS
    row_zero = (lax.axis_index("gy") * lax.axis_size("gz") + lax.axis_index("gz")) * nblk
    parent_row = parent[0]
    mine = lax.dynamic_slice_in_dim(parent_row, row_zero, nblk)
    links = link[:, 0, 0, :].T
    width = shell.shape[2] // 2

    def selector(piece):
        count = piece.shape[1]
        onehot = (mine[:, None] == jnp.arange(count, dtype=jnp.int32)[None, :]).astype(jnp.float32)
        return jnp.dot(
            onehot, piece[0], precision=lax.Precision.HIGHEST, preferred_element_type=jnp.float32
        )

    level_now = selector(lax.all_gather(shell[:, :, :width], ("gy", "gz"), axis=1, tiled=True))
    owner_mid = 0.5 * (shell[:, :, :width] + shell[:, :, width:])
    level_mid = selector(lax.all_gather(owner_mid, ("gy", "gz"), axis=1, tiled=True))
    state = fine
    for step in range(2):
        level = (level_now if step == 0 else level_mid).reshape(nblk, 6, 5, half, half)
        padded = padded_2(state, (("gx", 1), ("gy", 2), ("gz", 3)), 1)
        ghost_x0 = side_ghost(padded[:, 0, 1:-1, 1:-1], level, links, 0, nz_dev)
        ghost_x1 = side_ghost(padded[:, -1, 1:-1, 1:-1], level, links, 1, nz_dev)
        ghost_y0 = side_ghost(padded[:, 1:-1, 0, 1:-1], level, links, 2, nz_dev)
        ghost_y1 = side_ghost(padded[:, 1:-1, -1, 1:-1], level, links, 3, nz_dev)
        ghost_z0 = end_ghost(padded[:, 1:-1, 1:-1, 0:nz_dev:BS], level, links, 4)
        ghost_z1 = end_ghost(padded[:, 1:-1, 1:-1, BS + 1 :: BS], level, links, 5)
        ext_x = jnp.concatenate([ghost_x0[:, None], state, ghost_x1[:, None]], axis=1)
        ext_y = jnp.concatenate([ghost_y0[:, :, None], state, ghost_y1[:, :, None]], axis=2)
        total = (
            along_axis(ext_x, 0) + along_axis(ext_y, 1) + along_blocks(state, ghost_z0, ghost_z1)
        )
        state = state - LAMBDA * total
    restricted = restrict_state(state, nblk)
    piece = lax.all_gather(restricted, ("gy", "gz"), axis=0, tiled=True)
    count = piece.shape[0]
    wanted = row_zero + jnp.arange(nblk, dtype=jnp.int32)
    onehot = (parent_row[None, :] == wanted[:, None]).astype(jnp.float32)
    gathered = jnp.dot(
        onehot, piece, precision=lax.Precision.HIGHEST, preferred_element_type=jnp.float32
    )
    coarse_new = gathered.reshape(1, nblk, restricted.shape[1])
    return (state, coarse_new)


def solution(mesh):
    return jax.shard_map(
        shards,
        mesh=mesh,
        in_specs=(
            P(None, "gx", "gy", "gz"),
            P("gx", ("gy", "gz"), None),
            P("gx", None),
            P(None, "gx", "gy", "gz"),
        ),
        out_specs=(P(None, "gx", "gy", "gz"), P("gx", ("gy", "gz"), None)),
        check_vma=False,
    )
```

profile of v0, /device:TPU:105, one launch (start us, length us, event | category | flops | bytes accessed | tf_op | source)
XLA Modules:
  0.0 840.2 jit_solution(8892528713839068950)
XLA Ops:
  7.2 1.5 add_multiply_fusion
  9.5 1.4 fusion.133
  11.0 2.5 collective-permute-start.1
  13.5 1.3 copy.446
  14.8 4.3 slice.630
  19.1 4.3 slice.617
  29.2 4.2 slice.628
  33.5 4.3 slice.603
  39.2 165.1 %all-gather.6.cloned.1.call-done = f32[1,512,1920]{2,1,0:T(8,128)} async-done(((f32[1,8,1920]{2,1,0:T(8,128)}), f32[1,512,1920]{2,1,0:T(8,128)}) %all-gather.6.cloned.1.call-update) | async-done | bytes 3932176 | tf_op jit(solution)/shard_map/all_gather | solution.py:142
  204.2 5.5 copy.447
  209.7 185.8 %all-gather.4.cloned.1.call-done = f32[1,512,1920]{2,1,0:T(8,128)} async-done(((f32[1,8,1920]{2,1,0:T(8,128)}), f32[1,512,1920]{2,1,0:T(8,128)}) %all-gather.4.cloned.1.call-update) | async-done | bytes 3932176 | tf_op jit(solution)/shard_map/all_gather | solution.py:140
  395.6 5.7 copy.402
  401.3 15.3 %fusion.119 = f32[8,6,5,8,8]{4,0,3,2,1:T(8,128)S(1)} fusion(f32[6,5,8,8,512]{4,3,2,1,0:T(8,128)} %bitcast.437, s32[8]{0:T(128)S(1)} %dynamic-slice_bitcast_fusion), kind=kOutput, calls=%fused_computation.287 | convolution fusion | flops 94375936 | bytes 3993632 | tf_op jit(solution)/shard_map/dot_general | solution.py:136
  416.6 13.5 %fusion.121 = f32[8,6,5,8,8]{4,0,3,2,1:T(8,128)S(1)} fusion(f32[6,5,8,8,512]{4,3,2,1,0:T(8,128)S(1)} %bitcast.438, s32[8]{0:T(128)S(1)} %dynamic-slice_bitcast_fusion), kind=kOutput, calls=%fused_computation.288 | convolution fusion | flops 94375936 | bytes 3993632 | tf_op jit(solution)/shard_map/dot_general | solution.py:136
  436.4 1.4 fusion.7
  442.3 1.2 copy.438
  444.9 1.2 copy.466
  452.1 4.4 collective-permute-done.3
  460.4 1.2 copy.429
  464.0 1.6 fusion.13
  466.2 1.9 copy.431
  468.1 1.8 copy.432
  469.9 4.2 pad_maximum_fusion
  474.1 7.1 slice.619
  481.2 7.1 slice.607
  488.3 1.2 bitcast_select_fusion.2
  492.5 3.1 broadcast_in_dim.226
  495.6 4.7 reshape.314
  500.2 1.6 multiply_subtract_fusion.2
  501.8 3.1 broadcast_in_dim.231
  504.9 4.7 reshape.317
  509.6 2.0 fusion.26
  512.9 1.3 collective-permute-start.6
  516.5 4.3 slice.708
  520.8 4.4 slice.696
  528.4 4.2 slice.706
  532.6 4.4 slice.683
  537.0 1.7 collective-permute-start.7
  538.8 1.9 collective-permute-done.7
  541.0 2.3 collective-permute-start.8
  543.7 1.4 fusion.5
  545.1 3.9 collective-permute-done.9
  552.2 1.3 copy.458
  554.1 2.4 collective-permute-start.11
  556.5 1.6 fusion.11
  558.2 1.6 collective-permute-done.10
  560.6 1.8 copy.461
  562.4 3.9 pad_maximum_fusion.1
  566.3 6.2 slice.697
  572.5 7.1 slice.686
  579.6 1.7 bitcast_select_fusion
  584.0 3.1 broadcast_in_dim.242
  587.1 4.7 reshape.332
  591.7 1.5 multiply_subtract_fusion
  593.2 3.1 broadcast_in_dim.245
  596.3 4.7 reshape.335
  601.0 1.6 fusion.31
  603.4 8.7 %copy.470 = f32[5,16,16,128]{0,3,2,1:T(8,128)} copy(f32[5,16,16,128]{3,1,2,0:T(8,128)S(1)} %fusion.19) | data formatting | bytes 1310720 | tf_op jit(solution)/shard_map/sub | solution.py:158
  612.0 13.3 %reduce_sum.109 = f32[5,8,8,8,8]{0,4,3,2,1:T(8,128)} reduce(f32[5,8,2,8,2,8,8,2]{0,7,6,5,4,3,2,1:T(2,128)} %bitcast.434, f32[]{:T(128)} %constant.33.clone.1), dimensions={2,4,7}, to_apply=%region_10.11 | reduce | flops 143360 | bytes 737284 | tf_op jit(solution)/shard_map/reduce_sum | solution.py:119
  625.3 1.8 multiply_bitcast_fusion
  627.1 4.8 copy.471
  631.8 2.6 reshape.337
  635.5 192.8 %all-gather.8.cloned.1.call-done = f32[512,2560]{1,0:T(8,128)} async-done(((f32[8,2560]{1,0:T(8,128)}), f32[512,2560]{1,0:T(8,128)}) %all-gather.8.cloned.1.call-update) | async-done | bytes 5242896 | tf_op jit(solution)/shard_map/all_gather | solution.py:160
  828.3 4.9 convolution_bitcast_fusion
  (331 shorter events, 51.6 us)
Async XLA Ops:
  7.2 197.1 %all-gather.6.cloned.1.call-start = ((), (), s32[]{:S(2)}) async-start(), calls=%async_computation.1 | async-start | bytes 3993600 | tf_op jit(solution)/shard_map/all_gather | solution.py:142
  8.7 386.8 %all-gather.4.cloned.1.call-start = ((), (), s32[]{:S(2)}) async-start(), calls=%async_computation | async-start | bytes 3993600 | tf_op jit(solution)/shard_map/all_gather | solution.py:140
  9.5 818.8 %all-gather.8.cloned.1.call-start = ((), (), s32[]{:S(2)}) async-start(), calls=%async_computation.2 | async-start | bytes 5324800 | tf_op jit(solution)/shard_map/all_gather | solution.py:160
  11.0 420.6 %collective-permute-start.1 = (f32[5,1,16,128]{3,1,2,0:T(1,128)}, f32[5,1,16,128]{3,1,2,0:T(1,128)S(1)}, u32[]{:S(2)}, u32[]{:S(2)}) collective-permute-start(f32[5,1,16,128]{3,1,2,0:T(1,128)} %bitcast.15), channel_id=1, source_target_pairs={{64,0},{128,64},{192,128},{0,192},{65,1},{129,65},{193,129},{1,193... | collective-permute-start | bytes 122888 | tf_op jit(solution)/shard_map/ppermute | solution.py:20
  13.5 420.2 %collective-permute-start = (f32[5,1,16,128]{3,1,2,0:T(1,128)}, f32[5,1,16,128]{3,1,2,0:T(1,128)S(1)}, u32[]{:S(2)}, u32[]{:S(2)}) collective-permute-start(f32[5,1,16,128]{3,1,2,0:T(1,128)} %bitcast.2), channel_id=1, source_target_pairs={{0,64},{64,128},{128,192},{192,0},{1,65},{65,129},{129,193},{193,1... | collective-permute-start | bytes 122888 | tf_op jit(solution)/shard_map/ppermute | solution.py:18
  28.1 9.7 %copy-start.56 = (s32[6,1,1,8]{3,2,1,0:T(1,128)S(1)}, s32[6,1,1,8]{3,2,1,0:T(1,128)}, u32[]{:S(2)}) copy-start(s32[6,1,1,8]{3,2,1,0:T(1,128)} %param.7) | copy-start | bytes 580
  28.1 11.0 %copy-start.57 = (s32[1,512]{1,0:T(1,128)S(1)}, s32[1,512]{1,0:T(1,128)}, u32[]{:S(2)}) copy-start(s32[1,512]{1,0:T(1,128)} %param.6) | copy-start | bytes 6148
  401.3 15.3 %copy-start = (f32[1920,512]{1,0:T(8,128)S(1)}, f32[1920,512]{1,0:T(8,128)}, u32[]{:S(2)}) copy-start(f32[1920,512]{1,0:T(8,128)} %copy.402) | copy-start | bytes 11796484
  431.6 27.5 %copy-start.22 = (f32[5,1,16,128]{3,1,2,0:T(1,128)}, f32[5,1,16,128]{3,1,2,0:T(1,128)S(1)}, u32[]{:S(2)}) copy-start(f32[5,1,16,128]{3,1,2,0:T(1,128)S(1)} %collective-permute-done.1) | copy-start | bytes 122884
  433.7 25.4 %copy-start.24 = (f32[5,1,16,128]{3,1,2,0:T(1,128)}, f32[5,1,16,128]{3,1,2,0:T(1,128)S(1)}, u32[]{:S(2)}) copy-start(f32[5,1,16,128]{3,1,2,0:T(1,128)S(1)} %collective-permute-done) | copy-start | bytes 122884
  435.5 15.8 %collective-permute-start.2 = (f32[5,18,1,128]{3,1,2,0:T(8,128)}, f32[5,18,1,128]{3,1,2,0:T(8,128)}, u32[]{:S(2)}, u32[]{:S(2)}) collective-permute-start(f32[5,18,1,128]{3,1,2,0:T(8,128)} %get-tuple-element.58), channel_id=1, source_target_pairs={{0,8},{8,16},{16,24},{24,32},{32,40},{40,48},{48,56},{56,0},{1,9},... | collective-permute-start | bytes 138248 | tf_op jit(solution)/shard_map/ppermute | solution.py:18
  436.4 2.2 copy-start.30
  444.1 1.9 copy-start.31
  448.4 2.3 copy-start.55
  450.7 5.8 collective-permute-start.3
  452.1 4.4 copy-start.48
  456.5 2.6 copy-start.44
  462.3 7.6 copy-start.23
  462.3 7.6 copy-start.25
  462.3 7.6 copy-start.45
  462.3 5.8 collective-permute-start.5
  463.0 3.3 collective-permute-start.4
  474.1 14.2 %copy-start.7 = (f32[8,5,16,16]{0,2,3,1:T(8,128)S(1)}, f32[8,5,16,16]{0,2,3,1:T(8,128)}, u32[]{:S(2)}) copy-start(f32[8,5,16,16]{0,2,3,1:T(8,128)} %copy.438) | copy-start | bytes 122884
  488.3 1.4 copy-start.34
  489.6 1.3 copy-start.6
  489.6 1.3 copy-start.8
  491.0 1.3 copy-start.11
  495.6 4.7 copy-start.9
  504.9 4.7 copy-start.1
  504.9 4.7 copy-start.15
  504.9 4.7 copy-start.37
  509.6 2.3 copy-start.2
  509.6 2.3 copy-start.19
  509.6 2.3 copy-start.58
  512.9 25.8 %collective-permute-start.6 = (f32[5,1,16,128]{3,1,2,0:T(1,128)S(1)}, f32[5,1,16,128]{3,1,2,0:T(1,128)S(1)}, u32[]{:S(2)}, u32[]{:S(2)}) collective-permute-start(f32[5,1,16,128]{3,1,2,0:T(1,128)S(1)} %get-tuple-element.72), channel_id=1, source_target_pairs={{0,64},{64,128},{128,192},{192,0},{1,65},{65,129},{129,193},{193,1... | collective-permute-start | bytes 122888 | tf_op jit(solution)/shard_map/ppermute | solution.py:18
  525.2 13.5 %copy-start.54 = (f32[5,1,16,128]{3,1,2,0:T(1,128)S(1)}, f32[5,1,16,128]{3,1,2,0:T(1,128)}, u32[]{:S(2)}) copy-start(f32[5,1,16,128]{3,1,2,0:T(1,128)} %reshape.320) | copy-start | bytes 122884
  526.3 14.4 %copy-start.53 = (f32[5,1,16,128]{3,1,2,0:T(1,128)S(1)}, f32[5,1,16,128]{3,1,2,0:T(1,128)}, u32[]{:S(2)}) copy-start(f32[5,1,16,128]{3,1,2,0:T(1,128)} %reshape.323) | copy-start | bytes 122884
  537.0 3.6 collective-permute-start.7
  538.7 12.9 %copy-start.26 = (f32[5,1,16,128]{3,1,2,0:T(1,128)}, f32[5,1,16,128]{3,1,2,0:T(1,128)S(1)}, u32[]{:S(2)}) copy-start(f32[5,1,16,128]{3,1,2,0:T(1,128)S(1)} %collective-permute-done.6) | copy-start | bytes 122884
  540.7 11.0 %copy-start.28 = (f32[5,1,16,128]{3,1,2,0:T(1,128)}, f32[5,1,16,128]{3,1,2,0:T(1,128)S(1)}, u32[]{:S(2)}) copy-start(f32[5,1,16,128]{3,1,2,0:T(1,128)S(1)} %collective-permute-done.7) | copy-start | bytes 122884
  541.0 4.1 collective-permute-start.8
  543.3 5.8 collective-permute-start.9
  543.7 1.4 copy-start.52
  543.7 5.4 copy-start.51
  545.1 6.6 copy-start.40
  545.1 3.9 copy-start.47
  549.1 2.6 copy-start.42
  554.1 8.3 copy-start.27
  554.1 8.3 copy-start.29
  554.1 8.3 copy-start.41
  554.1 8.3 copy-start.43
  554.1 6.5 collective-permute-start.11
  556.5 3.2 collective-permute-start.10
  579.6 1.9 copy-start.36
  582.3 1.3 copy-start.13
  582.3 1.5 copy-start.14
  587.1 4.7 copy-start.12
  587.1 4.7 copy-start.39
  596.3 4.7 copy-start.16
  596.3 4.7 copy-start.17
  596.3 4.7 copy-start.38
  601.0 1.9 copy-start.3
  601.0 1.9 copy-start.18
  601.0 1.9 copy-start.59
  (11 other events, 9.8 us)
Sparse Core Ops, SparseCore 0:
  10.4 193.8 all-gather.5
  206.1 189.4 all-gather.3
  634.6 193.6 all-gather.7
where the time goes:
time: 846 us; the launch traced here: 840 us
  waiting for transfers between devices  557 us (66%)
  local copies, waits for them, and re-layouts  169 us (20%)
  other arithmetic  52.7 us (6%)
  matrix products  33.7 us (4%)
  between operations  15.5 us (2%)
  starting transfers between devices  12.5 us (1%)
    all_gather x1, waiting for transfers between devices, shards(): piece = lax.all_gather(restricted, ('gy', 'gz'), axis=0, tiled=True)  193 us
    all_gather x1, waiting for transfers between devices, shards(): lax.all_gather(shell[:, :, :width], ('gy', 'gz'), axis=1, tiled=True)  186 us
    all_gather x1, waiting for transfers between devices, shards(): lax.all_gather(owner_mid, ('gy', 'gz'), axis=1, tiled=True)  165 us
    dot_general x2, matrix products, selector(): jnp.dot(onehot, piece[0], precision=lax.Precision.HIGHEST, preferred_elem...  28.8 us
  transfers between devices with their start and end apart: 15, of which 8 were waited for; matrix products, arithmetic and copies ran while one was open for 14% of the time, Pallas kernels for 0%

commit v1 on v0

--- a/solution.py
+++ b/solution.py
@@ -6,6 +6,11 @@
 BS = 16
 GAMMA = 1.4
 LAMBDA = 0.05
+
+
+def swapped_in(x, axis, dim):
+    repeated = jnp.stack([x] * lax.axis_size(axis))
+    return jnp.concatenate(lax.all_to_all(repeated, axis, 0, 0), axis=dim)
 
 
 def padded_2(cells, sides, width):
@@ -137,7 +142,7 @@
             onehot, piece[0], precision=lax.Precision.HIGHEST, preferred_element_type=jnp.float32
         )
 
-    level_now = selector(lax.all_gather(shell[:, :, :width], ("gy", "gz"), axis=1, tiled=True))
+    level_now = selector(swapped_in(shell[:, :, :width], ("gy", "gz"), 1))
     owner_mid = 0.5 * (shell[:, :, :width] + shell[:, :, width:])
     level_mid = selector(lax.all_gather(owner_mid, ("gy", "gz"), axis=1, tiled=True))
     state = fine

time: 846 us -> 692 us (0.82)
  waiting for transfers between devices: 557 us -> 384 us
  starting transfers between devices: 12.5 us -> 23.8 us
    all_gather x1 -> x0, waiting for transfers between devices: 186 us -> none  [shards(): lax.all_gather(shell[:, :, :width], ('gy', 'gz'), axis=1, tiled=True)]
    all_gather x1, waiting for transfers between devices: 165 us -> 179 us  [shards(): lax.all_gather(owner_mid, ('gy', 'gz'), axis=1, tiled=True)]
    all_to_all x0 -> x1, starting transfers between devices: none -> 11.4 us  [swapped_in(): return jnp.concatenate(lax.all_to_all(repeated, axis, 0, 0), axis=dim)]
  transfers between devices with their start and end apart: 15 -> 15, of which waited for: 8 -> 7; matrix products, arithmetic and copies ran while one was open for 14% -> 18% of each run, Pallas kernels for 0% -> 0%
where the time goes in v1:
time: 692 us; the launch traced here: 685 us
  waiting for transfers between devices  384 us (55%)
  local copies, waits for them, and re-layouts  175 us (25%)
  other arithmetic  52.6 us (8%)
  matrix products  34.7 us (5%)
  starting transfers between devices  23.8 us (3%)
  between operations  15.8 us (2%)
    all_gather x1, waiting for transfers between devices, shards(): piece = lax.all_gather(restricted, ('gy', 'gz'), axis=0, tiled=True)  193 us
    all_gather x1, waiting for transfers between devices, shards(): lax.all_gather(owner_mid, ('gy', 'gz'), axis=1, tiled=True)  179 us
    dot_general x2, matrix products, selector(): jnp.dot(onehot, piece[0], precision=lax.Precision.HIGHEST, preferred_elem...  29.9 us
    slice x2, local copies, waits for them, and re-layouts, shards(): ghost_z1 = end_ghost(padded[:, 1:-1, 1:-1, BS + 1::BS], level, links, 5)  14.2 us
  transfers between devices with their start and end apart: 15, of which 7 were waited for; matrix products, arithmetic and copies ran while one was open for 18% of the time, Pallas kernels for 0%

profile of v1, /device:TPU:105, one launch (start us, length us, event | category | flops | bytes accessed | tf_op | source)
XLA Modules:
  0.0 685.5 jit_solution(4618734804135309588)
XLA Ops:
  7.2 1.5 add_multiply_fusion
  8.7 2.2 stack.22
  10.9 11.4 %all-to-all-start = ((f32[64,1,8,1920]{3,2,1,0:T(8,128)}), f32[64,1,8,1920]{3,2,1,0:T(8,128)}, u32[]{:S(2)}, u32[]{:S(2)}) async-start(f32[64,1,8,1920]{3,2,1,0:T(8,128)} %stack.22), calls=%async_computation | async-start | bytes 7864320 | tf_op jit(solution)/shard_map/all_to_all | solution.py:13
  23.0 2.5 collective-permute-start.1
  25.7 4.3 slice.633
  30.0 4.4 slice.620
  39.6 4.3 slice.631
  43.9 4.4 slice.606
  50.6 179.5 %all-gather.3.cloned.1.call-done = f32[1,512,1920]{2,1,0:T(8,128)} async-done(((f32[1,8,1920]{2,1,0:T(8,128)}), f32[1,512,1920]{2,1,0:T(8,128)}) %all-gather.3.cloned.1.call-update) | async-done | bytes 3932176 | tf_op jit(solution)/shard_map/all_gather | solution.py:147
  230.0 5.4 copy.447
  235.5 5.8 copy.402
  241.3 16.3 %fusion.119 = f32[8,6,5,8,8]{4,0,3,2,1:T(8,128)} fusion(f32[6,5,8,8,512]{4,3,2,1,0:T(8,128)} %bitcast.439, s32[8]{0:T(128)S(1)} %dynamic-slice_bitcast_fusion), kind=kOutput, calls=%fused_computation.288 | convolution fusion | flops 94375936 | bytes 3993632 | tf_op jit(solution)/shard_map/dot_general | solution.py:141
  257.6 13.5 %fusion.121 = f32[8,6,5,8,8]{4,0,3,2,1:T(8,128)S(1)} fusion(f32[6,5,8,8,512]{4,3,2,1,0:T(8,128)S(1)} %bitcast.440, s32[8]{0:T(128)S(1)} %dynamic-slice_bitcast_fusion), kind=kOutput, calls=%fused_computation.289 | convolution fusion | flops 94375936 | bytes 3993632 | tf_op jit(solution)/shard_map/dot_general | solution.py:141
  276.6 1.4 fusion.7
  295.2 4.4 collective-permute-done.3
  302.5 1.7 fusion.129
  304.2 1.9 copy.429
  306.1 1.9 copy.430
  308.0 1.6 collective-permute-start.4
  309.6 1.5 fusion.13
  311.2 1.8 copy.431
  313.0 1.8 copy.432
  314.9 4.3 pad_maximum_fusion
  319.1 7.0 %slice.622 = f32[5,16,16,8]{3,1,2,0:T(8,128)} slice(f32[5,18,18,130]{3,1,2,0:T(8,128)} %pad_maximum_fusion), slice={[0:5:1], [1:17:1], [1:17:1], [0:128:16]} | slice | bytes 81920 | tf_op jit(solution)/shard_map/slice | solution.py:156
  326.1 7.1 %slice.610 = f32[5,16,16,8]{3,1,2,0:T(8,128)} slice(f32[5,18,18,130]{3,1,2,0:T(8,128)} %pad_maximum_fusion), slice={[0:5:1], [1:17:1], [1:17:1], [17:130:16]} | slice | bytes 81920 | tf_op jit(solution)/shard_map/slice | solution.py:157
  333.2 1.4 bitcast_select_fusion.2
  338.0 3.1 broadcast_in_dim.226
  341.1 4.7 reshape.317
  345.7 1.7 multiply_subtract_fusion.2
  347.4 3.1 broadcast_in_dim.231
  350.5 4.7 reshape.320
  355.2 1.9 fusion.26
  358.4 1.3 collective-permute-start.6
  362.1 4.3 slice.711
  366.4 4.3 slice.699
  373.9 4.3 slice.709
  378.2 4.4 slice.686
  382.6 1.7 collective-permute-start.7
  384.3 1.3 collective-permute-done.7
  386.0 2.6 collective-permute-start.8
  389.0 1.4 fusion.5
  390.4 3.9 collective-permute-done.9
  397.5 1.2 copy.458
  399.4 2.0 collective-permute-start.11
  401.4 1.5 fusion.11
  403.0 1.7 collective-permute-done.10
  405.5 1.8 copy.461
  407.4 3.9 pad_maximum_fusion.1
  411.3 6.2 slice.700
  417.5 7.1 %slice.689 = f32[5,16,16,8]{3,1,2,0:T(8,128)} slice(f32[5,18,18,130]{3,1,2,0:T(8,128)} %pad_maximum_fusion.1), slice={[0:5:1], [1:17:1], [1:17:1], [17:130:16]} | slice | bytes 81920 | tf_op jit(solution)/shard_map/slice | solution.py:157
  424.5 1.7 bitcast_select_fusion
  429.0 3.1 broadcast_in_dim.242
  432.0 4.7 reshape.335
  436.7 1.5 multiply_subtract_fusion
  438.2 3.1 broadcast_in_dim.245
  441.2 4.7 reshape.338
  446.0 1.6 fusion.31
  448.3 8.8 %copy.470 = f32[5,16,16,128]{0,3,2,1:T(8,128)} copy(f32[5,16,16,128]{3,1,2,0:T(8,128)S(1)} %fusion.19) | data formatting | bytes 1310720 | tf_op jit(solution)/shard_map/sub | solution.py:163
  457.1 13.3 %reduce_sum.109 = f32[5,8,8,8,8]{0,4,3,2,1:T(8,128)} reduce(f32[5,8,2,8,2,8,8,2]{0,7,6,5,4,3,2,1:T(2,128)} %bitcast.436, f32[]{:T(128)} %constant.33.clone.1), dimensions={2,4,7}, to_apply=%region_10.11 | reduce | flops 143360 | bytes 737284 | tf_op jit(solution)/shard_map/reduce_sum | solution.py:124
  470.3 1.8 multiply_bitcast_fusion
  472.1 4.8 copy.471
  476.9 2.6 reshape.340
  480.6 192.8 %all-gather.5.cloned.1.call-done = f32[512,2560]{1,0:T(8,128)} async-done(((f32[8,2560]{1,0:T(8,128)}), f32[512,2560]{1,0:T(8,128)}) %all-gather.5.cloned.1.call-update) | async-done | bytes 5242896 | tf_op jit(solution)/shard_map/all_gather | solution.py:165
  673.3 4.9 convolution_bitcast_fusion
  (315 shorter events, 53.4 us)
Async XLA Ops:
  7.2 222.9 %all-gather.3.cloned.1.call-start = ((), (), s32[]{:S(2)}) async-start(), calls=%async_computation.1 | async-start | bytes 3993600 | tf_op jit(solution)/shard_map/all_gather | solution.py:147
  10.9 11.5 %copy-start.1 = (f32[5,16,16,128]{3,2,1,0:T(8,128)S(1)}, f32[5,16,16,128]{3,2,1,0:T(8,128)}, u32[]{:S(2)}) copy-start(f32[5,16,16,128]{3,2,1,0:T(8,128)} %param.4) | copy-start | bytes 1966084
  10.9 224.6 %all-to-all-start = ((f32[64,1,8,1920]{3,2,1,0:T(8,128)}), f32[64,1,8,1920]{3,2,1,0:T(8,128)}, u32[]{:S(2)}, u32[]{:S(2)}) async-start(f32[64,1,8,1920]{3,2,1,0:T(8,128)} %stack.22), calls=%async_computation | async-start | bytes 7864320 | tf_op jit(solution)/shard_map/all_to_all | solution.py:13
  22.3 651.0 %all-gather.5.cloned.1.call-start = ((), (), s32[]{:S(2)}) async-start(), calls=%async_computation.2 | async-start | bytes 5324800 | tf_op jit(solution)/shard_map/all_gather | solution.py:165
  23.0 249.5 %collective-permute-start.1 = (f32[5,1,16,128]{3,1,2,0:T(1,128)S(1)}, f32[5,1,16,128]{3,1,2,0:T(1,128)S(1)}, u32[]{:S(2)}, u32[]{:S(2)}) collective-permute-start(f32[5,1,16,128]{3,1,2,0:T(1,128)S(1)} %bitcast.470), channel_id=1, source_target_pairs={{64,0},{128,64},{192,128},{0,192},{65,1},{129,65},{193,129},{1,193... | collective-permute-start | bytes 122888 | tf_op jit(solution)/shard_map/ppermute | solution.py:25
  25.4 249.2 %collective-permute-start = (f32[5,1,16,128]{3,1,2,0:T(1,128)}, f32[5,1,16,128]{3,1,2,0:T(1,128)S(1)}, u32[]{:S(2)}, u32[]{:S(2)}) collective-permute-start(f32[5,1,16,128]{3,1,2,0:T(1,128)} %bitcast.2), channel_id=1, source_target_pairs={{0,64},{64,128},{128,192},{192,0},{1,65},{65,129},{129,193},{193,1... | collective-permute-start | bytes 122888 | tf_op jit(solution)/shard_map/ppermute | solution.py:23
  38.5 9.8 %copy-start.47 = (s32[6,1,1,8]{3,2,1,0:T(1,128)S(1)}, s32[6,1,1,8]{3,2,1,0:T(1,128)}, u32[]{:S(2)}) copy-start(s32[6,1,1,8]{3,2,1,0:T(1,128)} %param.7) | copy-start | bytes 580
  38.5 12.0 %copy-start.48 = (s32[1,512]{1,0:T(1,128)S(1)}, s32[1,512]{1,0:T(1,128)}, u32[]{:S(2)}) copy-start(s32[1,512]{1,0:T(1,128)} %param.6) | copy-start | bytes 6148
  241.3 16.4 %copy-start = (f32[1920,512]{1,0:T(8,128)S(1)}, f32[1920,512]{1,0:T(8,128)}, u32[]{:S(2)}) copy-start(f32[1920,512]{1,0:T(8,128)} %copy.402) | copy-start | bytes 11796484
  276.2 18.2 %collective-permute-start.2 = (f32[5,18,1,128]{3,1,2,0:T(8,128)}, f32[5,18,1,128]{3,1,2,0:T(8,128)}, u32[]{:S(2)}, u32[]{:S(2)}) collective-permute-start(f32[5,18,1,128]{3,1,2,0:T(8,128)} %get-tuple-element.58), channel_id=1, source_target_pairs={{0,8},{8,16},{16,24},{24,32},{32,40},{40,48},{48,56},{56,0},{1,9},... | collective-permute-start | bytes 138248 | tf_op jit(solution)/shard_map/ppermute | solution.py:23
  276.6 1.4 copy-start.4
  292.7 1.1 copy-start.46
  293.8 5.9 collective-permute-start.3
  295.2 4.5 copy-start.37
  300.6 0.9 copy-start.5
  304.2 5.4 copy-start.38
  304.2 5.4 copy-start.41
  308.0 5.1 collective-permute-start.5
  308.0 3.2 collective-permute-start.4
  333.2 1.6 copy-start.25
  334.6 1.8 copy-start.7
  334.6 1.8 copy-start.8
  336.5 1.1 copy-start.9
  336.5 1.3 copy-start.10
  341.1 4.7 copy-start.30
  350.5 4.7 copy-start.14
  350.5 4.7 copy-start.28
  355.1 2.2 copy-start.2
  355.2 2.2 copy-start.18
  355.2 2.2 copy-start.51
  358.4 25.8 %collective-permute-start.6 = (f32[5,1,16,128]{3,1,2,0:T(1,128)S(1)}, f32[5,1,16,128]{3,1,2,0:T(1,128)S(1)}, u32[]{:S(2)}, u32[]{:S(2)}) collective-permute-start(f32[5,1,16,128]{3,1,2,0:T(1,128)S(1)} %get-tuple-element.72), channel_id=1, source_target_pairs={{0,64},{64,128},{128,192},{192,0},{1,65},{65,129},{129,193},{193,1... | collective-permute-start | bytes 122888 | tf_op jit(solution)/shard_map/ppermute | solution.py:23
  370.7 13.5 %copy-start.45 = (f32[5,1,16,128]{3,1,2,0:T(1,128)S(1)}, f32[5,1,16,128]{3,1,2,0:T(1,128)}, u32[]{:S(2)}) copy-start(f32[5,1,16,128]{3,1,2,0:T(1,128)} %reshape.323) | copy-start | bytes 122884
  370.7 13.5 %copy-start.50 = (pred[128]{0:T(512)(128)(4,1)S(1)}, pred[128]{0:T(512)(128)(4,1)}, u32[]{:S(2)}) copy-start(pred[128]{0:T(512)(128)(4,1)} %broadcast_in_dim.203) | copy-start | bytes 388
  371.8 13.9 %copy-start.44 = (f32[5,1,16,128]{3,1,2,0:T(1,128)S(1)}, f32[5,1,16,128]{3,1,2,0:T(1,128)}, u32[]{:S(2)}) copy-start(f32[5,1,16,128]{3,1,2,0:T(1,128)} %reshape.326) | copy-start | bytes 122884
  371.8 13.9 %copy-start.49 = (pred[128]{0:T(512)(128)(4,1)S(1)}, pred[128]{0:T(512)(128)(4,1)}, u32[]{:S(2)}) copy-start(pred[128]{0:T(512)(128)(4,1)} %broadcast_in_dim.208) | copy-start | bytes 388
  382.6 3.0 collective-permute-start.7
  384.3 12.7 %copy-start.21 = (f32[5,1,16,128]{3,1,2,0:T(1,128)}, f32[5,1,16,128]{3,1,2,0:T(1,128)S(1)}, u32[]{:S(2)}) copy-start(f32[5,1,16,128]{3,1,2,0:T(1,128)S(1)} %collective-permute-done.6) | copy-start | bytes 122884
  385.6 11.3 %copy-start.23 = (f32[5,1,16,128]{3,1,2,0:T(1,128)}, f32[5,1,16,128]{3,1,2,0:T(1,128)S(1)}, u32[]{:S(2)}) copy-start(f32[5,1,16,128]{3,1,2,0:T(1,128)S(1)} %collective-permute-done.7) | copy-start | bytes 122884
  386.0 4.4 collective-permute-start.8
  388.6 5.8 collective-permute-start.9
  389.0 1.4 copy-start.43
  389.0 5.4 copy-start.42
  390.4 6.6 copy-start.32
  390.4 3.9 copy-start.36
  394.3 2.6 copy-start.34
  395.4 0.9 copy-start.6
  399.4 8.0 %copy-start.22 = (f32[5,1,16,128]{3,1,2,0:T(1,128)S(1)}, f32[5,1,16,128]{3,1,2,0:T(1,128)}, u32[]{:S(2)}) copy-start(f32[5,1,16,128]{3,1,2,0:T(1,128)} %copy-done.21) | copy-start | bytes 122884
  399.4 8.0 %copy-start.24 = (f32[5,1,16,128]{3,1,2,0:T(1,128)S(1)}, f32[5,1,16,128]{3,1,2,0:T(1,128)}, u32[]{:S(2)}) copy-start(f32[5,1,16,128]{3,1,2,0:T(1,128)} %copy-done.23) | copy-start | bytes 122884
  399.4 8.0 %copy-start.33 = (f32[5,18,1,128]{3,1,2,0:T(8,128)S(1)}, f32[5,18,1,128]{3,1,2,0:T(8,128)}, u32[]{:S(2)}) copy-start(f32[5,18,1,128]{3,1,2,0:T(8,128)} %copy-done.32) | copy-start | bytes 138244
  399.4 8.0 %copy-start.35 = (f32[5,18,1,128]{3,1,2,0:T(8,128)S(1)}, f32[5,18,1,128]{3,1,2,0:T(8,128)}, u32[]{:S(2)}) copy-start(f32[5,18,1,128]{3,1,2,0:T(8,128)} %copy-done.34) | copy-start | bytes 138244
  399.4 6.1 collective-permute-start.11
  401.4 3.3 collective-permute-start.10
  424.5 1.9 copy-start.27
  426.4 1.0 copy-start.26
  427.2 0.9 copy-start.20
  427.2 1.3 copy-start.12
  427.2 1.5 copy-start.13
  432.0 4.7 copy-start.11
  432.0 4.7 copy-start.31
  441.2 4.7 copy-start.15
  441.2 4.7 copy-start.16
  441.2 4.7 copy-start.29
  446.0 1.9 copy-start.3
  446.0 1.9 copy-start.17
  (3 other events, 2.1 us)
Sparse Core Ops, SparseCore 0:
  10.4 219.6 all-gather.2
  479.6 193.6 all-gather.4
